TPU v7x, 256 devices: a whole 4x4x8 slice. The times are simulated.
256 devices in a mesh: row: 8 (over z), col: 32 (over y, x, core).
Axes of the slice: x: 4, y: 4, z: 8, core: 2. Of those that a mesh axis runs over, the one named last changes fastest.
Arguments:
- hidden_in: bfloat16 [1024, 2304], P('row', 'col'), may hold values from -40 to 40
- attn_gain: float32 [2304], P('col'), may hold values from 0.1 to 1.9
- qkv_weight: bfloat16 [2304, 6912], P('col'), may hold values from -0.125 to 0.125
- out_weight: bfloat16 [2304, 2304], P(None, 'col'), may hold values from -0.125 to 0.125
- moe_gain: float32 [2304], P('col'), may hold values from 0.1 to 1.9
- router_weight: float32 [2304, 8], P('col'), may hold values from -0.125 to 0.125
- expert_gate: bfloat16 [8, 2304, 5760], P('row', None, 'col'), may hold values from -0.125 to 0.125
- expert_up: bfloat16 [8, 2304, 5760], P('row', None, 'col'), may hold values from -0.125 to 0.125
- expert_down: bfloat16 [8, 5760, 2304], P('row', 'col'), may hold values from -0.078125 to 0.078125
- cache_keys: bfloat16 [2048, 64, 2304], P(('row', 'col')), may hold values from -400 to 400
- cache_values: bfloat16 [2048, 64, 2304], P(('row', 'col')), may hold values from -12 to 12
- block_table: int32 [8, 4, 64], P('row'), may hold values from 0 to 2047, as said below
- prefix_lengths: int32 [8, 4], P('row'), may hold values from 1024 to 4096, as said below
- prompt_lengths: int32 [8, 4], P('row'), may hold values from 1 to 64, 128 in all within a row
- routed_experts: int32 [1024, 2], P('row'), may hold values from 0 to 7, all different within a row; in each aligned block of 128 rows (0 to 127, 128 to 255, ...) at most 64 rows name the same one
Outputs:
- attn_out: bfloat16 [1024, 2304], P('row', 'col')
- moe_out: bfloat16 [1024, 2304], P('row', 'col')
- layer_out: bfloat16 [1024, 2304], P('row', 'col')
Inputs may be any that keep to these rules, and one draw needn't show every extreme that they name: `block_table`: entry [g, q, j] lies among the 8 pages that begin at (g * 32 + j % 32) * 8; the entries that fall among the same 8 pages are distinct. `prefix_lengths`: some request has exactly 4096 cached tokens. `prompt_lengths`: the 4 lengths of a group sum to 128; the longest of each group is exactly 64. `routed_experts`: the 2 experts of a token differ; among the tokens of one group no expert is named more than 64 times, and in some group an expert reaches 64; every expert is named by some token.
All inputs are finite; a program needn't handle non-finite values.
Results may differ from a plain program's by a relative error of at most 0.02.
The roundings to bfloat16 on the way count: a program that leaves them out, or rounds other values in their place, can miss the bound.
Values may be sent and summed in bfloat16 or wider, within the bound.
No kernel may reach another device: no remote copies, remote signals or barrier semaphores. Data moves between devices by JAX's collectives and lax.ppermute only.
A program may use at most 192 MiB of HBM per device.

v0:
```python
import math
import jax
import jax.numpy as jnp
from jax import lax
from jax.sharding import PartitionSpec as P

D = 2304
HEAD_DIM = 64
TOP = 2
norm_epsilon = 1e-05
residual_scale = 1.4 / math.sqrt(40.0)
rotary_base = 10000.0
masked_score = -1e30


def merged(value, axis, join):
    pieces = jax.tree.map(lambda part: lax.all_gather(part, axis), value)
    head = jax.tree.map(lambda part: part[0], pieces)
    tail = jax.tree.map(lambda part: part[1:], pieces)
    running, _ = lax.scan(lambda running, slab: (join(running, slab), None), head, tail)
    return running


def rotate(values, positions, head_dim):
    row_count = values.shape[0]
    head_count = values.shape[1] // head_dim
    half_dim = head_dim // 2
    frequency = rotary_base ** (-2.0 * jnp.arange(half_dim, dtype=jnp.float32) / head_dim)
    angles = positions.astype(jnp.float32)[:, None] * frequency[None, :]
    cosine = jnp.cos(angles)[:, None, :]
    sine_part = jnp.sin(angles)[:, None, :]
    shaped = values.reshape(row_count, head_count, head_dim)
    first_half = shaped[:, :, :half_dim]
    second_half = shaped[:, :, half_dim:]
    turned = jnp.concatenate(
        [
            first_half * cosine - second_half * sine_part,
            second_half * cosine + first_half * sine_part,
        ],
        axis=2,
    )
    return turned.reshape(row_count, head_count * head_dim)


def token_layout(prompt_row, prefix_row, row_count):
    run_ends = jnp.cumsum(prompt_row, dtype=jnp.int32)
    starts = run_ends - prompt_row
    offsets = jnp.arange(row_count, dtype=jnp.int32)
    request = jnp.sum(
        (offsets[:, None] >= run_ends[None, :]).astype(jnp.int32), axis=1, dtype=jnp.int32
    )
    member = request[:, None] == jnp.arange(prompt_row.shape[0], dtype=jnp.int32)[None, :]
    start_of = jnp.sum(jnp.where(member, starts[None, :], 0), axis=1, dtype=jnp.int32)
    prefix_of = jnp.sum(jnp.where(member, prefix_row[None, :], 0), axis=1, dtype=jnp.int32)
    return (request, prefix_of + offsets - start_of)


def rescale(summed, factor):
    group_count, row_count, feature_width = summed.shape
    group_size = factor.shape[1]
    shaped = summed.reshape(group_count, row_count, group_size, feature_width // group_size)
    shaped = shaped * jnp.transpose(factor, (0, 2, 1))[:, :, :, None]
    return shaped.reshape(group_count, row_count, feature_width)


def divide_rows(summed, total_weight):
    group_count, row_count, feature_width = summed.shape
    group_size = total_weight.shape[1]
    shaped = summed.reshape(group_count, row_count, group_size, feature_width // group_size)
    shaped = shaped / jnp.transpose(total_weight, (0, 2, 1))[:, :, :, None]
    return shaped.reshape(group_count, row_count, feature_width)


def combine_parts(earlier_part, later_part):
    largest = jnp.maximum(earlier_part[0], later_part[0])
    factor_one = jnp.exp(earlier_part[0] - largest)
    factor_two = jnp.exp(later_part[0] - largest)
    total_weight = earlier_part[1] * factor_one + later_part[1] * factor_two
    summed = rescale(earlier_part[2], factor_one) + rescale(later_part[2], factor_two)
    return (largest, total_weight, summed)


def on_device(
    hidden_in,
    attn_gain,
    qkv_weight,
    out_weight,
    moe_gain,
    router_weight,
    expert_gate,
    expert_up,
    expert_down,
    cache_keys,
    cache_values,
    block_table,
    prefix_lengths,
    prompt_lengths,
    routed_experts,
):
    col_count = lax.axis_size("col")
    row_devices = lax.axis_size("row")
    col_index = lax.axis_index("col")
    row_index = lax.axis_index("row")
    tok_rows = hidden_in.shape[0]
    feature_width = hidden_in.shape[1]
    head_total = out_weight.shape[0]
    head_count = head_total // HEAD_DIM
    key_share = tok_rows // col_count
    request, position = token_layout(prompt_lengths[0], prefix_lengths[0], tok_rows)
    own_start = col_index * key_share
    key_position = lax.dynamic_slice_in_dim(position, own_start, key_share)
    key_request = lax.dynamic_slice_in_dim(request, own_start, key_share)
    residual = hidden_in.astype(jnp.float32)
    squares = lax.psum(jnp.sum(residual * residual, axis=1), "col")
    scale_one = lax.rsqrt(squares / D + norm_epsilon)
    normed = (residual * scale_one[:, None] * attn_gain[None, :]).astype(jnp.bfloat16)
    query_part = jnp.dot(normed, qkv_weight[:, :head_total], preferred_element_type=jnp.float32)
    query_sum = lax.psum(query_part, "col")
    queries = (rotate(query_sum, position, HEAD_DIM) * HEAD_DIM ** (-0.5)).astype(jnp.bfloat16)
    key_value = lax.psum_scatter(
        jnp.dot(normed, qkv_weight[:, head_total:], preferred_element_type=jnp.float32).astype(
            jnp.bfloat16
        ),
        "col",
        scatter_dimension=0,
        tiled=True,
    ).astype(jnp.float32)
    new_keys = rotate(key_value[:, :head_total], key_position, HEAD_DIM).astype(jnp.bfloat16)
    new_values = key_value[:, head_total:].astype(jnp.bfloat16)
    pool_size = cache_keys.shape[0]
    page_size = cache_keys.shape[1]
    req_count = block_table.shape[1]
    pages_each = block_table.shape[2] // col_count
    page_table = block_table[0].reshape(req_count, pages_each, col_count)
    own_pages = lax.dynamic_slice_in_dim(page_table, col_index, 1, 2).reshape(
        req_count * pages_each
    )
    pool_offset_begin = (row_index * col_count + col_index) * pool_size
    slot_ids = jnp.arange(pool_size, dtype=jnp.int32)
    entry_ids = jnp.arange(req_count * pages_each, dtype=jnp.int32)
    slot_match = (own_pages - pool_offset_begin)[None, :] == slot_ids[:, None]
    entry_request = entry_ids // pages_each
    entry_page = entry_ids % pages_each * col_count + col_index
    slot_request = jnp.sum(
        jnp.where(slot_match, entry_request[None, :], 0), axis=1, dtype=jnp.int32
    )
    slot_page = jnp.sum(jnp.where(slot_match, entry_page[None, :], 0), axis=1, dtype=jnp.int32)
    prefix_row = prefix_lengths[0]
    slot_prefix = jnp.sum(
        jnp.where(
            slot_request[:, None] == jnp.arange(req_count, dtype=jnp.int32)[None, :],
            prefix_row[None, :],
            0,
        ),
        axis=1,
        dtype=jnp.int32,
    )
    cache_position = (
        slot_page[:, None] * page_size + jnp.arange(page_size, dtype=jnp.int32)[None, :]
    )
    cache_live = (
        (cache_position < slot_prefix[:, None]).astype(jnp.int32).reshape(pool_size * page_size)
    )
    cache_request = jnp.broadcast_to(slot_request[:, None], (pool_size, page_size)).reshape(
        pool_size * page_size
    )
    cache_mask = (request[:, None] == cache_request[None, :]) & (cache_live[None, :] > 0)
    fresh_mask = (request[:, None] == key_request[None, :]) & (
        key_position[None, :] <= position[:, None]
    )
    group_size = math.gcd(head_count, 4)
    group_count = head_count // group_size
    query_heads = queries.reshape(tok_rows, head_count, HEAD_DIM)
    cached_key_heads = cache_keys.reshape(pool_size * page_size, head_count, HEAD_DIM)
    cached_value_heads = cache_values.reshape(pool_size * page_size, head_count, HEAD_DIM)
    fresh_key_heads = new_keys.reshape(key_share, head_count, HEAD_DIM)
    fresh_value_heads = new_values.reshape(key_share, head_count, HEAD_DIM)

    def head_group(group_index):
        first_head = group_index * group_size
        query_piece = lax.dynamic_slice_in_dim(query_heads, first_head, group_size, 1)
        key_piece = lax.dynamic_slice_in_dim(cached_key_heads, first_head, group_size, 1)
        value_piece = lax.dynamic_slice_in_dim(cached_value_heads, first_head, group_size, 1)
        fresh_key_piece = lax.dynamic_slice_in_dim(fresh_key_heads, first_head, group_size, 1)
        fresh_value_piece = lax.dynamic_slice_in_dim(fresh_value_heads, first_head, group_size, 1)
        score_matrix = jnp.einsum(
            "thd,khd->htk", query_piece, key_piece, preferred_element_type=jnp.float32
        )
        score_matrix = jnp.where(cache_mask[None], score_matrix, masked_score)
        fresh_scores = jnp.einsum(
            "thd,khd->htk", query_piece, fresh_key_piece, preferred_element_type=jnp.float32
        )
        fresh_scores = jnp.where(fresh_mask[None], fresh_scores, masked_score)
        largest = jnp.maximum(jnp.max(score_matrix, axis=2), jnp.max(fresh_scores, axis=2))
        cached_exp = jnp.where(cache_mask[None], jnp.exp(score_matrix - largest[:, :, None]), 0.0)
        fresh_exp = jnp.where(fresh_mask[None], jnp.exp(fresh_scores - largest[:, :, None]), 0.0)
        total_weight = jnp.sum(cached_exp, axis=2) + jnp.sum(fresh_exp, axis=2)
        summed = jnp.einsum(
            "htk,khd->thd",
            cached_exp.astype(jnp.bfloat16),
            value_piece,
            preferred_element_type=jnp.float32,
        )
        summed = summed + jnp.einsum(
            "htk,khd->thd",
            fresh_exp.astype(jnp.bfloat16),
            fresh_value_piece,
            preferred_element_type=jnp.float32,
        )
        return (largest, total_weight, summed.reshape(tok_rows, group_size * HEAD_DIM))

    largest, total_weight, summed = lax.map(head_group, jnp.arange(group_count, dtype=jnp.int32))
    largest, total_weight, summed = merged((largest, total_weight, summed), "col", combine_parts)
    attended = divide_rows(summed, total_weight).astype(jnp.bfloat16)
    projected = jnp.einsum(
        "gtx,gxo->to",
        attended,
        out_weight.reshape(group_count, group_size * HEAD_DIM, feature_width),
        preferred_element_type=jnp.float32,
    )
    attn_out = projected.astype(jnp.bfloat16)
    middle = (residual + residual_scale * attn_out.astype(jnp.float32)).astype(jnp.bfloat16)
    middle_wide = middle.astype(jnp.float32)
    squares_two = lax.psum(jnp.sum(middle_wide * middle_wide, axis=1), "col")
    scale_two = lax.rsqrt(squares_two / D + norm_epsilon)
    moe_normed_f = middle_wide * scale_two[:, None] * moe_gain[None, :]
    logits = lax.psum(jnp.dot(moe_normed_f, router_weight, precision=lax.Precision.HIGHEST), "col")
    moe_normed = moe_normed_f.astype(jnp.bfloat16)
    expert_local = expert_gate.shape[0]
    expert_total = expert_local * row_devices
    capacity = 2 * TOP * tok_rows // expert_total
    onehot_three = (
        routed_experts[:, :, None] == jnp.arange(expert_total, dtype=jnp.int32)[None, None, :]
    )
    selected_logits = jnp.sum(jnp.where(onehot_three, logits[:, None, :], 0.0), axis=2)
    first_gate = jax.nn.sigmoid(selected_logits[:, 0] - selected_logits[:, 1])
    gate_pair = jnp.stack([first_gate, 1.0 - first_gate], axis=1)
    onehot = onehot_three.astype(jnp.int32).reshape(tok_rows * TOP, expert_total)
    earlier = jnp.cumsum(onehot, axis=0, dtype=jnp.int32) - onehot
    slot_index = jnp.sum(earlier * onehot, axis=1, dtype=jnp.int32)
    target = routed_experts.reshape(tok_rows * TOP) * capacity + slot_index
    token_local = jnp.arange(tok_rows * TOP, dtype=jnp.int32) // TOP
    source = jnp.zeros((expert_total * capacity,), jnp.int32).at[target].set(token_local)
    filled = jnp.zeros((expert_total * capacity,), jnp.int32).at[target].set(1)
    outgoing = jnp.where(
        filled[:, None] > 0, moe_normed[source], jnp.zeros((), jnp.bfloat16)
    ).reshape(expert_total, capacity, feature_width)
    arrived = lax.all_to_all(outgoing, "row", split_axis=0, concat_axis=0, tiled=True)
    expert_rows = (
        arrived.reshape(row_devices, expert_local, capacity, feature_width)
        .transpose(1, 0, 2, 3)
        .reshape(expert_local, row_devices * capacity, feature_width)
    )
    feature_piece = lax.all_gather(expert_rows, "col", axis=2, tiled=True)
    gate_next = jnp.einsum(
        "erd,edf->erf", feature_piece, expert_gate, preferred_element_type=jnp.float32
    )
    up_next = jnp.einsum(
        "erd,edf->erf", feature_piece, expert_up, preferred_element_type=jnp.float32
    )
    hidden = (jax.nn.silu(gate_next) * up_next).astype(jnp.bfloat16)
    received_rows = hidden.shape[1]
    value_partial_sum = jnp.einsum(
        "efo,erf->oer", expert_down, hidden, preferred_element_type=jnp.float32
    )
    expert_out = lax.psum_scatter(
        value_partial_sum.reshape(
            lax.axis_size("col") * feature_width, expert_local * received_rows
        ).astype(jnp.bfloat16),
        "col",
        scatter_dimension=0,
        tiled=True,
    )
    returned = lax.all_to_all(
        expert_out.reshape(feature_width, expert_local, received_rows),
        "row",
        split_axis=2,
        concat_axis=1,
        tiled=True,
    )
    flat_back = returned.reshape(feature_width, expert_total * capacity)
    picked = (
        jnp.take(flat_back, target, axis=1)
        .astype(jnp.float32)
        .reshape(feature_width, tok_rows, TOP)
    )
    moe_columns = jnp.sum(picked * gate_pair[None, :, :], axis=2).astype(jnp.bfloat16)
    moe_out = moe_columns.T
    layer_out = (middle_wide + residual_scale * moe_out.astype(jnp.float32)).astype(jnp.bfloat16)
    return (attn_out, moe_out, layer_out)


def solution(mesh):
    in_specs = (
        P("row", "col"),
        P("col"),
        P("col", None),
        P(None, "col"),
        P("col"),
        P("col", None),
        P("row", None, "col"),
        P("row", None, "col"),
        P("row", "col", None),
        P(("row", "col"), None, None),
        P(("row", "col"), None, None),
        P("row", None, None),
        P("row", None),
        P("row", None),
        P("row", None),
    )
    out_specs = (P("row", "col"), P("row", "col"), P("row", "col"))
    return jax.shard_map(
        on_device, mesh=mesh, in_specs=in_specs, out_specs=out_specs, check_vma=False
    )
```

profile of v0, /device:TPU:2, one launch (start us, length us, event | category | flops | bytes accessed | tf_op | source)
XLA Modules:
  0.0 942.3 jit_solution(6926186442801343392)
XLA Ops:
  8.0 62.3 %psum.28 = f32[128]{0:T(128)S(1)} all-reduce(f32[128]{0:T(128)S(1)} %fusion.64), channel_id=1, replica_groups=mesh['row'=8,'col'=32] {'col'}, use_global_device_ids=true, to_apply=%region_1.2 | all-reduce | flops 128 | bytes 1024 | tf_op jit(solution)/shard_map/psum | solution.py:114
  70.3 2.7 convolution_convert_fusion
  77.7 5.0 reshape.454
  82.7 6.9 copy.162
  89.5 5.0 reshape.455
  94.5 6.7 copy.163
  102.5 88.4 %all-reduce.6.cloned.1.call-done = bf16[128,4608]{1,0:T(8,128)(2,1)} async-done(((bf16[128,4608]{1,0:T(8,128)(2,1)}), bf16[128,4608]{1,0:T(8,128)(2,1)}) %all-reduce.6.cloned.1.call-update) | async-done | bytes 1179664
  192.2 117.1 %all-reduce.4.cloned.1.call-done = f32[128,36,64]{0,2,1:T(8,128)} async-done(((f32[128,36,64]{0,2,1:T(8,128)}), f32[128,36,64]{0,2,1:T(8,128)}) %all-reduce.4.cloned.1.call-update) | async-done | bytes 1179664 | tf_op jit(solution)/shard_map/psum | solution.py:118
  310.9 51.9 %while.31 = (s32[]{:T(128)}, f32[9,4,128]{2,1,0:T(4,128)S(1)}, f32[9,4,128]{2,1,0:T(4,128)S(1)}, f32[9,128,256]{2,1,0:T(8,128)}, s32[9]{0:T(128)S(1)}, /*index=5...) while((s32[]{:T(128)}, f32[9,4,128]{2,1,0:T(4,128)S(1)}, ...), condition=%wide.region_16.17_spmd.clone.clone, body=%wide.region_11.16_spmd.clone.clone.sunk | while | flops 69911040 | bytes 5058339 | solution.py:212
  368.0 24.4 %all-gather = f32[288,4,128]{2,1,0:T(4,128)S(1)} all-gather(f32[9,4,128]{2,1,0:T(4,128)S(1)} %get-tuple-element.105), channel_id=2, replica_groups=mesh['row'=8,'col'=32] {'col'}, dimensions={0}, use_global_device_ids=true | all-gather | bytes 608256 | tf_op jit(solution)/shard_map/all_gather | solution.py:17
  392.5 25.6 %all-gather.1 = f32[288,4,128]{2,1,0:T(4,128)S(1)} all-gather(f32[9,4,128]{2,1,0:T(4,128)S(1)} %get-tuple-element.106), channel_id=3, replica_groups=mesh['row'=8,'col'=32] {'col'}, dimensions={0}, use_global_device_ids=true | all-gather | bytes 608256 | tf_op jit(solution)/shard_map/all_gather | solution.py:17
  418.2 76.0 %all-gather.8.cloned.1.call-done = f32[288,128,256]{2,1,0:T(8,128)} async-done(((f32[9,128,256]{2,1,0:T(8,128)}), f32[288,128,256]{2,1,0:T(8,128)}) %all-gather.8.cloned.1.call-update) | async-done | bytes 37748752 | tf_op jit(solution)/shard_map/all_gather | solution.py:17
  496.8 26.9 %slice.93 = f32[279,128,256]{2,1,0:T(8,128)} slice(f32[288,128,256]{2,1,0:T(8,128)} %all-gather.8.cloned.1.call-done), slice={[9:288], [0:128], [0:256]} | slice | bytes 73138176 | tf_op jit(solution)/shard_map/slice | solution.py:19
  523.7 168.2 %while.30 = (s32[]{:T(128)}, f32[9,4,128]{2,1,0:T(4,128)S(1)}, f32[9,4,128]{2,1,0:T(4,128)S(1)}, f32[9,128,256]{1,2,0:T(8,128)}, f32[31,9,4,128]{3,2,1,0:T(4,128...) while((s32[]{:T(128)}, f32[9,4,128]{2,1,0:T(4,128)S(1)}, ...), condition=%wide.region_18.19_spmd, body=%wide.region_17.18_spmd.sunk | while | flops 916994 | bytes 17676496 | solution.py:20
  531.9 2.6 fusion.111
  694.2 60.6 %psum.30 = f32[128]{0:T(128)S(1)} all-reduce(f32[128]{0:T(128)S(1)} %get-tuple-element.401), channel_id=1, replica_groups=mesh['row'=8,'col'=32] {'col'}, use_global_device_ids=true, to_apply=%region_24.25 | all-reduce | flops 128 | bytes 1024 | tf_op jit(solution)/shard_map/psum | solution.py:224
  756.5 15.9 %all_to_all.14 = bf16[8,64,72]{2,1,0:T(8,128)(2,1)S(1)} all-to-all(bf16[8,64,72]{2,1,0:T(8,128)(2,1)S(1)} %broadcast_select_fusion), channel_id=1, replica_groups=mesh['row'=8,'col'=32] {'row'}, dimensions={0} | all-to-all | bytes 147456 | tf_op jit(solution)/shard_map/all_to_all | solution.py:248
  773.2 44.9 %all-gather.6.cloned.1.call-done = bf16[1,512,2304]{1,2,0:T(8,128)(2,1)} async-done(((bf16[1,512,72]{1,2,0:T(8,128)(2,1)}), bf16[1,512,2304]{1,2,0:T(8,128)(2,1)}) %all-gather.6.cloned.1.call-update) | async-done | bytes 2359312 | tf_op jit(solution)/shard_map/all_gather | solution.py:254
  818.1 3.0 fusion.36
  821.2 3.4 fusion.33
  827.9 60.4 %psum.31 = f32[128,8]{0,1:T(8,128)S(1)} all-reduce(f32[128,8]{0,1:T(8,128)S(1)} %fusion.70), channel_id=1, replica_groups=mesh['row'=8,'col'=32] {'col'}, use_global_device_ids=true, to_apply=%region_27.28 | all-reduce | flops 1024 | bytes 8192 | tf_op jit(solution)/shard_map/psum | solution.py:227
  888.4 25.3 %reduce-scatter.4.cloned.1.call-done = bf16[72,512]{1,0:T(8,128)(2,1)} async-done(((bf16[2304,512]{1,0:T(8,128)(2,1)}), bf16[72,512]{1,0:T(8,128)(2,1)}) %reduce-scatter.4.cloned.1.call-update) | async-done | bytes 73744
  917.8 7.0 all-to-all-start.1
  925.0 8.3 all-to-all-done.1
  (695 shorter events, 240.1 us)
Async XLA Ops:
  7.2 814.0 %copy-start = (bf16[1,180,2304]{2,1,0:T(8,128)(2,1)S(1)}, bf16[1,180,2304]{2,1,0:T(8,128)(2,1)}, u32[]{:S(2)}) copy-start(bf16[1,180,2304]{2,1,0:T(8,128)(2,1)} %param.27) | copy-start | bytes 2488324
  7.2 183.7 %all-reduce.6.cloned.1.call-start = ((), (), s32[]{:S(2)}) async-start(), calls=%async_computation.7 | async-start | bytes 2359296
  70.3 2.9 copy-start.8
  70.3 2.9 copy-start.12
  73.1 2.9 copy-start.17
  73.1 3.2 copy-start.14
  73.1 3.4 copy-start.11
  73.1 4.6 copy-start.1
  73.1 236.2 %all-reduce.4.cloned.1.call-start = ((), (), s32[]{:S(2)}) async-start(), calls=%async_computation.3 | async-start | bytes 2359296 | tf_op jit(solution)/shard_map/psum | solution.py:118
  75.8 418.3 %all-gather.8.cloned.1.call-start = ((), (), s32[]{:S(2)}) async-start(), calls=%async_computation.5 | async-start | bytes 38928384 | tf_op jit(solution)/shard_map/all_gather | solution.py:17
  82.7 6.9 copy-start.2
  94.5 6.7 copy-start.18
  362.8 455.3 %all-gather.6.cloned.1.call-start = ((), (), s32[]{:S(2)}) async-start(), calls=%async_computation.4 | async-start | bytes 2433024 | tf_op jit(solution)/shard_map/all_gather | solution.py:254
  526.5 2.6 copy-start.4
  531.9 2.6 copy-start.4
  537.3 2.6 copy-start.4
  542.8 2.6 copy-start.4
  548.2 2.6 copy-start.4
  553.6 2.6 copy-start.4
  651.3 2.6 copy-start.4
  691.9 62.9 %copy-start.13 = (f32[72]{0:T(128)S(1)}, f32[72]{0:T(128)}, u32[]{:S(2)}) copy-start(f32[72]{0:T(128)} %param.23) | copy-start | bytes 868
  694.2 123.9 %copy-start.15 = (bf16[1,2304,180]{1,2,0:T(8,128)(2,1)S(1)}, bf16[1,2304,180]{1,2,0:T(8,128)(2,1)}, u32[]{:S(2)}) copy-start(bf16[1,2304,180]{1,2,0:T(8,128)(2,1)} %param.25) | copy-start | bytes 2488324
  773.1 140.5 %reduce-scatter.4.cloned.1.call-start = ((), (), s32[]{:S(2)}) async-start(), calls=%async_computation.6 | async-start | bytes 2433024
  917.8 15.5 %all-to-all-start.1 = ((bf16[8,2,2304]{2,1,0:T(2,128)(2,1)}), bf16[8,2,2304]{2,1,0:T(2,128)(2,1)S(1)}, u32[]{:S(2)}, u32[]{:S(2)}) async-start(bf16[8,2,2304]{2,1,0:T(2,128)(2,1)} %reshape.465), calls=%async_computation.1 | async-start | bytes 147456 | tf_op jit(solution)/shard_map/all_to_all | solution.py:274
  (122 other events, 206.0 us)
Sparse Core Ops, SparseCore 0:
  73.2 117.6 all-reduce.5
  194.2 115.0 all-reduce.3
  362.9 131.1 all-gather.7
  773.3 44.8 all-gather.5
  827.2 86.4 reduce-scatter.3
where the time goes:
time: 946 us; the launch traced here: 942 us
  waiting for transfers between devices  360 us (38%)
  blocking collectives  249 us (26%)
  local copies, waits for them, and re-layouts  164 us (17%)
  other arithmetic  97.8 us (10%)
  matrix products  40.8 us (4%)
  between operations  14.9 us (2%)
    psum x1, waiting for transfers between devices, on_device(): query_sum = lax.psum(query_part, 'col')  117 us
    unnamed x7, waiting for transfers between devices  114 us
    add x31, other arithmetic, combine_parts(): rescale(earlier_part[2], factor_one) + rescale(later_part[2], factor_two)  81.3 us
    all_gather x1, waiting for transfers between devices, merged(): pieces = jax.tree.map(lambda part: lax.all_gather(part, axis), value)  76 us
    psum x1, blocking collectives, on_device(): squares = lax.psum(jnp.sum(residual * residual, axis=1), 'col')  62.3 us
    psum x1, blocking collectives, on_device(): squares_two = lax.psum(jnp.sum(middle_wide * middle_wide, axis=1), 'col')  60.6 us
    psum x1, blocking collectives, on_device(): lax.psum(jnp.dot(moe_normed_f, router_weight, precision=lax.Precision.HIG...  60.4 us
    dynamic_slice x62, local copies, waits for them, and re-layouts, merged(): lax.scan(lambda running, slab: (join(running, slab), None), head, tail)  53.9 us
  transfers between devices with their start and end apart: 6, of which 6 were waited for; matrix products, arithmetic and copies ran while one was open for 4% of the time, Pallas kernels for 0%

commit v1 on v0

--- a/solution.py
+++ b/solution.py
@@ -221,7 +221,7 @@
     attn_out = projected.astype(jnp.bfloat16)
     middle = (residual + residual_scale * attn_out.astype(jnp.float32)).astype(jnp.bfloat16)
     middle_wide = middle.astype(jnp.float32)
-    squares_two = lax.psum(jnp.sum(middle_wide * middle_wide, axis=1), "col")
+    squares_two = jnp.sum(lax.all_gather(jnp.sum(middle_wide * middle_wide, axis=1), "col"), axis=0)
     scale_two = lax.rsqrt(squares_two / D + norm_epsilon)
     moe_normed_f = middle_wide * scale_two[:, None] * moe_gain[None, :]
     logits = lax.psum(jnp.dot(moe_normed_f, router_weight, precision=lax.Precision.HIGHEST), "col")

time: 946 us -> 905 us (0.957)
  blocking collectives: 249 us -> 210 us
    psum x1 -> x0, blocking collectives: 60.6 us -> none  [on_device(): squares_two = lax.psum(jnp.sum(middle_wide * middle_wide, axis=1), 'col')]
    all_gather x0 -> x1, blocking collectives: none -> 20.6 us  [on_device(): lax.all_gather(jnp.sum(middle_wide * middle_wide, axis=1), 'col')]
where the time goes in v1:
time: 905 us; the launch traced here: 902 us
  waiting for transfers between devices  359 us (40%)
  blocking collectives  210 us (23%)
  local copies, waits for them, and re-layouts  163 us (18%)
  other arithmetic  97.8 us (11%)
  matrix products  40.8 us (5%)
  between operations  14.9 us (2%)
    psum x1, waiting for transfers between devices, on_device(): query_sum = lax.psum(query_part, 'col')  117 us
    unnamed x7, waiting for transfers between devices  114 us
    add x31, other arithmetic, combine_parts(): rescale(earlier_part[2], factor_one) + rescale(later_part[2], factor_two)  81.3 us
    all_gather x1, waiting for transfers between devices, merged(): pieces = jax.tree.map(lambda part: lax.all_gather(part, axis), value)  76 us
    psum x1, blocking collectives, on_device(): squares = lax.psum(jnp.sum(residual * residual, axis=1), 'col')  62.3 us
    psum x1, blocking collectives, on_device(): lax.psum(jnp.dot(moe_normed_f, router_weight, precision=lax.Precision.HIG...  60.5 us
    dynamic_slice x62, local copies, waits for them, and re-layouts, merged(): lax.scan(lambda running, slab: (join(running, slab), None), head, tail)  53.9 us
    all_gather x2, blocking collectives, merged(): pieces = jax.tree.map(lambda part: lax.all_gather(part, axis), value)  50.1 us
  transfers between devices with their start and end apart: 6, of which 6 were waited for; matrix products, arithmetic and copies ran while one was open for 4% of the time, Pallas kernels for 0%

profile of v1, /device:TPU:2, one launch (start us, length us, event | category | flops | bytes accessed | tf_op | source)
XLA Modules:
  0.0 901.8 jit_solution(3761320331663184024)
XLA Ops:
  8.0 62.3 %psum.21 = f32[128]{0:T(128)S(1)} all-reduce(f32[128]{0:T(128)S(1)} %fusion.64), channel_id=1, replica_groups=mesh['row'=8,'col'=32] {'col'}, use_global_device_ids=true, to_apply=%region_1.2 | all-reduce | flops 128 | bytes 1024 | tf_op jit(solution)/shard_map/psum | solution.py:114
  70.3 2.7 convolution_convert_fusion
  77.7 5.0 reshape.462
  82.7 6.9 copy.162
  89.5 5.0 reshape.463
  94.5 6.7 copy.163
  102.5 88.4 %all-reduce.6.cloned.1.call-done = bf16[128,4608]{1,0:T(8,128)(2,1)} async-done(((bf16[128,4608]{1,0:T(8,128)(2,1)}), bf16[128,4608]{1,0:T(8,128)(2,1)}) %all-reduce.6.cloned.1.call-update) | async-done | bytes 1179664
  192.2 117.1 %all-reduce.4.cloned.1.call-done = f32[128,36,64]{0,2,1:T(8,128)} async-done(((f32[128,36,64]{0,2,1:T(8,128)}), f32[128,36,64]{0,2,1:T(8,128)}) %all-reduce.4.cloned.1.call-update) | async-done | bytes 1179664 | tf_op jit(solution)/shard_map/psum | solution.py:118
  310.9 51.9 %while.31 = (s32[]{:T(128)}, f32[9,4,128]{2,1,0:T(4,128)S(1)}, f32[9,4,128]{2,1,0:T(4,128)S(1)}, f32[9,128,256]{2,1,0:T(8,128)}, s32[9]{0:T(128)S(1)}, /*index=5...) while((s32[]{:T(128)}, f32[9,4,128]{2,1,0:T(4,128)S(1)}, ...), condition=%wide.region_16.17_spmd.clone.clone, body=%wide.region_11.16_spmd.clone.clone.sunk | while | flops 69911040 | bytes 5058339 | solution.py:212
  368.0 24.4 %all-gather = f32[288,4,128]{2,1,0:T(4,128)S(1)} all-gather(f32[9,4,128]{2,1,0:T(4,128)S(1)} %get-tuple-element.105), channel_id=2, replica_groups=mesh['row'=8,'col'=32] {'col'}, dimensions={0}, use_global_device_ids=true | all-gather | bytes 608256 | tf_op jit(solution)/shard_map/all_gather | solution.py:17
  392.5 25.6 %all-gather.1 = f32[288,4,128]{2,1,0:T(4,128)S(1)} all-gather(f32[9,4,128]{2,1,0:T(4,128)S(1)} %get-tuple-element.106), channel_id=3, replica_groups=mesh['row'=8,'col'=32] {'col'}, dimensions={0}, use_global_device_ids=true | all-gather | bytes 608256 | tf_op jit(solution)/shard_map/all_gather | solution.py:17
  418.2 76.0 %all-gather.10.cloned.1.call-done = f32[288,128,256]{2,1,0:T(8,128)} async-done(((f32[9,128,256]{2,1,0:T(8,128)}), f32[288,128,256]{2,1,0:T(8,128)}) %all-gather.10.cloned.1.call-update) | async-done | bytes 37748752 | tf_op jit(solution)/shard_map/all_gather | solution.py:17
  496.8 26.9 %slice.93 = f32[279,128,256]{2,1,0:T(8,128)} slice(f32[288,128,256]{2,1,0:T(8,128)} %all-gather.10.cloned.1.call-done), slice={[9:288], [0:128], [0:256]} | slice | bytes 73138176 | tf_op jit(solution)/shard_map/slice | solution.py:19
  523.7 168.2 %while.30 = (s32[]{:T(128)}, f32[9,4,128]{2,1,0:T(4,128)S(1)}, f32[9,4,128]{2,1,0:T(4,128)S(1)}, f32[9,128,256]{1,2,0:T(8,128)}, f32[31,9,4,128]{3,2,1,0:T(4,128...) while((s32[]{:T(128)}, f32[9,4,128]{2,1,0:T(4,128)S(1)}, ...), condition=%wide.region_18.19_spmd, body=%wide.region_17.18_spmd.sunk | while | flops 916994 | bytes 17676496 | solution.py:20
  531.9 2.6 fusion.111
  694.2 20.6 %all-gather.4 = f32[32,1,128]{2,1,0:T(1,128)S(1)} all-gather(f32[1,1,128]{2,1,0:T(1,128)S(1)} %bitcast.165), channel_id=5, replica_groups=mesh['row'=8,'col'=32] {'col'}, dimensions={0}, use_global_device_ids=true | all-gather | bytes 16896 | tf_op jit(solution)/shard_map/all_gather | solution.py:224
  716.6 16.4 %all_to_all.14 = bf16[8,64,72]{2,1,0:T(8,128)(2,1)S(1)} all-to-all(bf16[8,64,72]{2,1,0:T(8,128)(2,1)S(1)} %broadcast_select_fusion), channel_id=1, replica_groups=mesh['row'=8,'col'=32] {'row'}, dimensions={0} | all-to-all | bytes 147456 | tf_op jit(solution)/shard_map/all_to_all | solution.py:248
  733.7 43.9 %all-gather.8.cloned.1.call-done = bf16[1,512,2304]{1,2,0:T(8,128)(2,1)} async-done(((bf16[1,512,72]{1,2,0:T(8,128)(2,1)}), bf16[1,512,2304]{1,2,0:T(8,128)(2,1)}) %all-gather.8.cloned.1.call-update) | async-done | bytes 2359312 | tf_op jit(solution)/shard_map/all_gather | solution.py:254
  777.7 3.0 fusion.36
  780.7 3.4 fusion.33
  787.4 60.5 %psum.23 = f32[128,8]{0,1:T(8,128)S(1)} all-reduce(f32[128,8]{0,1:T(8,128)S(1)} %fusion.70), channel_id=1, replica_groups=mesh['row'=8,'col'=32] {'col'}, use_global_device_ids=true, to_apply=%region_27.28 | all-reduce | flops 1024 | bytes 8192 | tf_op jit(solution)/shard_map/psum | solution.py:227
  847.9 25.3 %reduce-scatter.4.cloned.1.call-done = bf16[72,512]{1,0:T(8,128)(2,1)} async-done(((bf16[2304,512]{1,0:T(8,128)(2,1)}), bf16[72,512]{1,0:T(8,128)(2,1)}) %reduce-scatter.4.cloned.1.call-update) | async-done | bytes 73744
  877.3 7.0 all-to-all-start.1
  884.5 8.3 all-to-all-done.1
  (696 shorter events, 240.2 us)
Async XLA Ops:
  7.2 773.5 %copy-start = (bf16[1,180,2304]{2,1,0:T(8,128)(2,1)S(1)}, bf16[1,180,2304]{2,1,0:T(8,128)(2,1)}, u32[]{:S(2)}) copy-start(bf16[1,180,2304]{2,1,0:T(8,128)(2,1)} %param.27) | copy-start | bytes 2488324
  7.2 183.7 %all-reduce.6.cloned.1.call-start = ((), (), s32[]{:S(2)}) async-start(), calls=%async_computation.7 | async-start | bytes 2359296
  70.3 2.9 copy-start.8
  70.3 2.9 copy-start.12
  73.1 2.9 copy-start.17
  73.1 3.2 copy-start.14
  73.1 3.4 copy-start.11
  73.1 4.6 copy-start.1
  73.1 236.2 %all-reduce.4.cloned.1.call-start = ((), (), s32[]{:S(2)}) async-start(), calls=%async_computation.3 | async-start | bytes 2359296 | tf_op jit(solution)/shard_map/psum | solution.py:118
  75.8 418.3 %all-gather.10.cloned.1.call-start = ((), (), s32[]{:S(2)}) async-start(), calls=%async_computation.5 | async-start | bytes 38928384 | tf_op jit(solution)/shard_map/all_gather | solution.py:17
  82.7 6.9 copy-start.2
  94.5 6.7 copy-start.18
  362.8 414.9 %all-gather.8.cloned.1.call-start = ((), (), s32[]{:S(2)}) async-start(), calls=%async_computation.4 | async-start | bytes 2433024 | tf_op jit(solution)/shard_map/all_gather | solution.py:254
  526.5 2.6 copy-start.4
  531.9 2.6 copy-start.4
  537.3 2.6 copy-start.4
  542.8 2.6 copy-start.4
  548.2 2.6 copy-start.4
  553.6 2.6 copy-start.4
  651.3 2.6 copy-start.4
  691.9 22.9 %copy-start.13 = (f32[72]{0:T(128)S(1)}, f32[72]{0:T(128)}, u32[]{:S(2)}) copy-start(f32[72]{0:T(128)} %param.23) | copy-start | bytes 868
  694.2 83.4 %copy-start.15 = (bf16[1,2304,180]{1,2,0:T(8,128)(2,1)S(1)}, bf16[1,2304,180]{1,2,0:T(8,128)(2,1)}, u32[]{:S(2)}) copy-start(bf16[1,2304,180]{1,2,0:T(8,128)(2,1)} %param.25) | copy-start | bytes 2488324
  733.7 139.5 %reduce-scatter.4.cloned.1.call-start = ((), (), s32[]{:S(2)}) async-start(), calls=%async_computation.6 | async-start | bytes 2433024
  877.3 15.5 %all-to-all-start.1 = ((bf16[8,2,2304]{2,1,0:T(2,128)(2,1)}), bf16[8,2,2304]{2,1,0:T(2,128)(2,1)S(1)}, u32[]{:S(2)}, u32[]{:S(2)}) async-start(bf16[8,2,2304]{2,1,0:T(2,128)(2,1)} %reshape.473), calls=%async_computation.1 | async-start | bytes 147456 | tf_op jit(solution)/shard_map/all_to_all | solution.py:274
  (122 other events, 206.0 us)
Sparse Core Ops, SparseCore 0:
  73.2 117.6 all-reduce.5
  194.2 115.0 all-reduce.3
  362.9 131.1 all-gather.9
  733.8 43.8 all-gather.7
  786.7 86.4 reduce-scatter.3
